TPU v7x, 32 devices: a whole 2x2x4 slice. The times are simulated.
32 devices in a mesh: tm: 16 (over z, x, core), doc: 2 (over y).
Axes of the slice: x: 2, y: 2, z: 4, core: 2. Of those that a mesh axis runs over, the one named last changes fastest.
Arguments:
- beta: float32 [16, 4096, 128], P('tm', 'doc'), may hold values from -6 to 260
- word_ids: int32 [16, 8, 128], P('tm', 'doc'), may hold values from 0 to 4095
- word_counts: int32 [16, 8, 128], P('tm', 'doc'), may hold values from 1 to 8
- block_slot: int32 [32], replicated, may hold values from 0 to 31, each once
- topic_prior: float32 [128], replicated, may hold values from 0.05 to 0.5
- drift_var: float32 [128], replicated, may hold values from 0.0005 to 0.05
- obs_precision: float32 [16, 128], replicated, may hold values from 0.01 to 4
Outputs:
- smoothed_means: float32 [16, 4096, 128], P('tm', 'doc')
- doc_topics: float32 [16, 8, 128], P('tm', 'doc')
Inputs may be any that keep to these rules, and one draw needn't show every extreme that they name: `block_slot`: each block has its own position.
All inputs are finite; a program needn't handle non-finite values.
Results may differ from a plain program's by a relative error of at most 0.0012.
The roundings to bfloat16 on the way count: a program that leaves them out, or rounds other values in their place, can miss the bound.
Values may be sent and summed in bfloat16 or wider, within the bound.
No kernel may reach another device: no remote copies, remote signals or barrier semaphores. Data moves between devices by JAX's collectives and lax.ppermute only.
A program may use at most 192 MiB of HBM per device.

v0:
```python
import jax
import jax.numpy as jnp
from jax import lax
from jax.sharding import PartitionSpec as P

K = 128
BLOCK = 128
EITERS = 4
init_variance = 4.0


def joined(value, axis, combine):
    everything = jax.tree.map(lambda part: lax.all_gather(part, axis), value)
    initial = jax.tree.map(lambda part: part[0], everything)

    def step(k, so_far):
        return combine(so_far, jax.tree.map(lambda part: part[k], everything))

    return lax.fori_loop(1, lax.axis_size(axis), step, initial)


def entering(part, axis, combine, identity, reverse):
    count = lax.axis_size(axis)
    place = lax.axis_index(axis)
    ahead = count - 1 - place if reverse else place
    gathered = jax.tree.map(lambda a: lax.all_gather(a, axis), part)
    state = jax.tree.map(lambda a, e: jnp.zeros_like(a) + jnp.asarray(e, a.dtype), part, identity)

    def one(step, state):
        source = count - 1 - step if reverse else step
        return combine(
            state, jax.tree.map(lambda a: lax.dynamic_index_in_dim(a, source, 0, False), gathered)
        )

    return lax.fori_loop(0, ahead, one, state)


def variance_tables(obs_precision, drift_var):

    def forward_step(prior_var, precision):
        denominator = 1.0 + prior_var * precision
        gain_now = prior_var * precision / denominator
        filt_var = prior_var / denominator
        return (filt_var + drift_var, (gain_now, filt_var))

    start_var = jnp.full(drift_var.shape, init_variance, dtype=jnp.float32)
    last_var, (gains, filt_vars) = lax.scan(forward_step, start_var, obs_precision)

    def backward_step(info_next, precision):
        merged = info_next + precision
        shrink = 1.0 / (1.0 + drift_var * merged)
        info_now = merged * shrink
        return (info_now, (shrink, info_now))

    zero_info = jnp.zeros(drift_var.shape, dtype=jnp.float32)
    last_info, (shrinks, infos) = lax.scan(
        backward_step, zero_info, obs_precision[1:], reverse=True
    )
    shrinks = jnp.concatenate([shrinks, jnp.ones_like(zero_info)[None]], axis=0)
    infos = jnp.concatenate([infos, zero_info[None]], axis=0)
    return (gains, filt_vars, shrinks, infos)


def e_step(looked, word_counts, topic_prior):
    counts_float = word_counts.astype(jnp.float32)
    doc_topics = topic_prior + jnp.sum(counts_float, axis=-1, keepdims=True) / K
    scores = looked.astype(jnp.float32)
    for sweep in range(EITERS):
        resp = jax.nn.softmax(lax.digamma(doc_topics)[..., None, :] + scores, axis=-1)
        doc_topics = topic_prior + jnp.sum(counts_float[..., None] * resp, axis=-2)
    weighted = (counts_float[..., None] * resp).astype(jnp.bfloat16)
    return (doc_topics, weighted)


def combine_normalizer(first_part, second_part):
    peak_value = jnp.maximum(first_part[0], second_part[0])
    summed = first_part[1] * jnp.exp(first_part[0] - peak_value) + second_part[1] * jnp.exp(
        second_part[0] - peak_value
    )
    return (peak_value, summed)


def compose_maps(earlier, later):
    return (later[0] * earlier[0], later[0] * earlier[1] + later[1])


def pick_year(table_all, year_index):
    return lax.dynamic_index_in_dim(table_all, year_index, 0, keepdims=False)


def body(beta, word_ids, word_counts, block_slot, topic_prior, drift_var, obs_precision):
    local_beta = beta[0]
    own_words = local_beta.shape[0]
    topics = local_beta.shape[1]
    local_peak = jnp.max(local_beta, axis=0)
    local_total = jnp.sum(jnp.exp(local_beta - local_peak), axis=0)
    peak_value, total_value = joined((local_peak, local_total), "doc", combine_normalizer)
    table = (local_beta - (peak_value + jnp.log(total_value))).astype(jnp.bfloat16)
    slot_ids = word_ids[0]
    doc_count = slot_ids.shape[0]
    slot_width = slot_ids.shape[1]
    block_count = block_slot.shape[0]
    block_of = slot_ids // BLOCK
    block_match = block_of[..., None] == lax.iota(jnp.int32, block_count)
    columns = jnp.sum(jnp.where(block_match, block_slot, 0), axis=-1) * BLOCK + slot_ids % BLOCK
    flat_columns = columns.reshape(-1)
    slot_total = flat_columns.shape[0]
    piece = lax.all_gather(table, "doc", axis=0, tiled=True)
    inside = (flat_columns >= 0) & (flat_columns < piece.shape[0])
    picked = jnp.take(piece, jnp.clip(flat_columns, 0, piece.shape[0] - 1), axis=0)
    looked = jnp.where(inside[:, None], picked, jnp.zeros_like(picked)).reshape(
        doc_count, slot_width, topics
    )
    doc_topics, weighted = e_step(looked, word_counts[0], topic_prior)
    flat_weighted = weighted.reshape(slot_total, topics)
    row_words = lax.iota(jnp.int32, own_words * lax.axis_size("doc"))
    marks = (row_words[:, None] == flat_columns[None, :]).astype(jnp.bfloat16)
    counts = lax.psum_scatter(
        jnp.dot(marks, flat_weighted, preferred_element_type=jnp.float32).astype(jnp.bfloat16),
        "doc",
        scatter_dimension=0,
        tiled=True,
    ).astype(jnp.float32)
    pseudo = local_beta + jnp.log1p(counts)
    gains, filt_vars, shrinks, infos = variance_tables(obs_precision, drift_var)
    year_index = lax.axis_index("tm")
    years_total = obs_precision.shape[0]
    gain_now = pick_year(gains, year_index)
    filt_now = pick_year(filt_vars, year_index)
    keep_part = 1.0 - gain_now
    push_part = gain_now * pseudo
    identity_map = (jnp.ones_like(keep_part), jnp.zeros_like(push_part))
    before = entering((keep_part, push_part), "tm", compose_maps, identity_map, False)
    filtered = keep_part * before[1] + push_part
    pull_now = jnp.where(year_index == years_total - 1, 0.0, filt_now / (filt_now + drift_var))
    own_term = (1.0 - pull_now) * filtered
    after = entering((pull_now, own_term), "tm", compose_maps, identity_map, True)
    smoothed = pull_now * after[1] + own_term
    return (smoothed[None], doc_topics[None])


def solution(mesh):
    in_specs = (
        P("tm", "doc", None),
        P("tm", "doc", None),
        P("tm", "doc", None),
        P(),
        P(),
        P(),
        P(),
    )
    out_specs = (P("tm", "doc", None), P("tm", "doc", None))
    return jax.shard_map(body, mesh=mesh, in_specs=in_specs, out_specs=out_specs, check_vma=False)
```

profile of v0, /device:TPU:0, one launch (start us, length us, event | category | flops | bytes accessed | tf_op | source)
XLA Modules:
  0.0 387.6 jit_solution(6193052944169842220)
XLA Ops:
  7.2 1.6 reduce_max.53
  10.3 5.2 %all-gather.8 = f32[2,1,128]{2,1,0:T(1,128)S(1)} all-gather(f32[1,1,128]{2,1,0:T(1,128)S(1)} %bitcast.211), channel_id=4, replica_groups=mesh['tm'=16,'doc'=2] {'doc'}, dimensions={0}, use_global_device_ids=true | all-gather | bytes 1536 | tf_op jit(solution)/shard_map/all_gather | solution.py:13
  15.5 4.2 %all-gather.7 = f32[2,1,128]{2,1,0:T(1,128)S(1)} all-gather(f32[1,1,128]{2,1,0:T(1,128)S(1)} %bitcast.210), channel_id=3, replica_groups=mesh['tm'=16,'doc'=2] {'doc'}, dimensions={0}, use_global_device_ids=true | all-gather | bytes 1536 | tf_op jit(solution)/shard_map/all_gather | solution.py:13
  19.8 2.1 fusion.6
  27.8 17.2 %all-gather.13.cloned.1.call-done = bf16[4096,128]{1,0:T(8,128)(2,1)} async-done(((bf16[2048,128]{1,0:T(8,128)(2,1)}), bf16[4096,128]{1,0:T(8,128)(2,1)}) %all-gather.13.cloned.1.call-update) | async-done | bytes 1048592 | tf_op jit(solution)/shard_map/all_gather | solution.py:108
  45.1 2.4 gather_fusion
  53.1 2.4 fusion.2
  55.6 12.5 %while.49 = (s32[]{:T(128)}, f32[128]{0:T(128)S(1)}, f32[16,128]{1,0:T(8,128)S(1)}, f32[16,128]{1,0:T(8,128)S(1)}, f32[16,128]{1,0:T(8,128)}, /*index=5*/f32[128]{0:T(128)S(1)}, s32[]{:T(128)}, s32[]{:T(128)}) while((s32[]{:T(128)}, f32[128]{0:T(128)S(1)}, f32[16,128]{1,0:T(8,128)S(1)}, f32[16,128]{1,0:T(8,128)S(1)}, ...), condition=%wide.region_1.0_spmd.clone, body=%wide.region_0.0_spmd.clone.sunk | while | flops 771 | bytes 5235 | solution.py:47
  68.1 7.9 %reduce-scatter.2.cloned.1.call-done = bf16[2048,128]{1,0:T(8,128)(2,1)} async-done(((bf16[4096,128]{1,0:T(8,128)(2,1)}), bf16[2048,128]{1,0:T(8,128)(2,1)}) %reduce-scatter.2.cloned.1.call-update) | async-done | bytes 524304 | tf_op jit(solution)/shard_map/reduce_scatter | solution.py:118
  76.0 2.4 fusion.7
  78.5 21.7 %all-gather.6 = f32[16,1,128]{2,1,0:T(1,128)S(1)} all-gather(f32[1,1,128]{2,1,0:T(1,128)S(1)} %get-tuple-element.251), channel_id=1, replica_groups=mesh['tm'=16,'doc'=2] {'tm'}, dimensions={0}, use_global_device_ids=true | all-gather | bytes 8704 | tf_op jit(solution)/shard_map/all_gather | solution.py:26
  100.3 105.0 %all-gather.15.cloned.1.call-done = f32[32768,128]{1,0:T(8,128)} async-done(((f32[2048,128]{1,0:T(8,128)}), f32[32768,128]{1,0:T(8,128)}) %all-gather.15.cloned.1.call-update) | async-done | bytes 16777232 | tf_op jit(solution)/shard_map/all_gather | solution.py:26
  207.6 40.6 %all-gather.5 = f32[16,1,128]{2,1,0:T(1,128)S(1)} all-gather(f32[1,1,128]{2,1,0:T(1,128)S(1)} %bitcast.209), channel_id=2, replica_groups=mesh['tm'=16,'doc'=2] {'tm'}, dimensions={0}, use_global_device_ids=true | all-gather | bytes 8704 | tf_op jit(solution)/shard_map/all_gather | solution.py:26
  249.2 106.2 %all-gather.17.cloned.1.call-done = f32[32768,128]{1,0:T(8,128)} async-done(((f32[2048,128]{1,0:T(8,128)}), f32[32768,128]{1,0:T(8,128)}) %all-gather.17.cloned.1.call-update) | async-done | bytes 16777232 | tf_op jit(solution)/shard_map/all_gather | solution.py:26
  355.5 24.4 %while.48 = (s32[]{:T(128)}, f32[2048,128]{1,0:T(8,128)S(1)}, s32[]{:T(128)}, f32[16,128]{1,0:T(8,128)S(1)}, f32[16,2048,128]{2,1,0:T(8,128)}, /*index=5*/s32[]{:T(128)}, s32[]{:T(128)}, s32[]{:T(128)}, s32[]{:T(128)}) while((s32[]{:T(128)}, f32[2048,128]{1,0:T(8,128)S(1)}, s32[]{:T(128)}, f32[16,128]{1,0:T(8,128)S(1)}, ...), condition=%wide.region_21.22_spmd, body=%wide.region_20.21_spmd.sunk | while | flops 524294 | bytes 3147419 | solution.py:35
  355.6 1.7 bitcast_add_fusion.8
  357.2 1.6 bitcast_add_fusion.8
  358.9 1.6 bitcast_add_fusion.8
  360.5 1.6 bitcast_add_fusion.8
  365.4 1.6 bitcast_add_fusion.8
  367.0 1.6 bitcast_add_fusion.8
  368.6 1.6 bitcast_add_fusion.8
  370.2 1.6 bitcast_add_fusion.8
  371.9 1.6 bitcast_add_fusion.8
  (130 shorter events, 39.5 us)
Async XLA Ops:
  7.2 68.9 %copy-start = (f32[1,2048,128]{2,1,0:T(8,128)S(1)}, f32[1,2048,128]{2,1,0:T(8,128)}, u32[]{:S(2)}) copy-start(f32[1,2048,128]{2,1,0:T(8,128)} %param.13) | copy-start | bytes 3145732
  7.2 48.4 %copy-start.3 = (f32[128]{0:T(128)S(1)}, f32[128]{0:T(128)}, u32[]{:S(2)}) copy-start(f32[128]{0:T(128)} %param.18) | copy-start | bytes 1540
  7.2 37.9 %all-gather.13.cloned.1.call-start = ((), (), s32[]{:S(2)}) async-start(), calls=%async_computation.1 | async-start | bytes 1572864 | tf_op jit(solution)/shard_map/all_gather | solution.py:108
  21.9 54.2 %reduce-scatter.2.cloned.1.call-start = ((), (), s32[]{:S(2)}) async-start(), calls=%async_computation.2 | async-start | bytes 1572864 | tf_op jit(solution)/shard_map/reduce_scatter | solution.py:118
  55.5 149.8 %all-gather.15.cloned.1.call-start = ((), (), s32[]{:S(2)}) async-start(), calls=%async_computation.3 | async-start | bytes 17825792 | tf_op jit(solution)/shard_map/all_gather | solution.py:26
  78.5 277.0 %all-gather.17.cloned.1.call-start = ((), (), s32[]{:S(2)}) async-start(), calls=%async_computation.4 | async-start | bytes 17825792 | tf_op jit(solution)/shard_map/all_gather | solution.py:26
  205.2 1.2 copy-start.2
  205.3 43.3 %copy-start.4 = (f32[128]{0:T(128)S(1)}, f32[128]{0:T(128)}, u32[]{:S(2)}) copy-start(f32[128]{0:T(128)} %param.17) | copy-start | bytes 1540
  355.4 24.5 %copy-start.1 = (f32[2048,128]{1,0:T(8,128)S(1)}, f32[2048,128]{1,0:T(8,128)}, u32[]{:S(2)}) copy-start(f32[2048,128]{1,0:T(8,128)} %add_multiply_fusion) | copy-start | bytes 3145732
Sparse Core Ops, SparseCore 0:
  22.0 23.0 all-gather.12
  55.6 20.3 reduce-scatter.1
  78.8 126.4 all-gather.14
  207.8 147.5 all-gather.16
where the time goes:
time: 389 us; the launch traced here: 388 us
  waiting for transfers between devices  236 us (61%)
  blocking collectives  71.7 us (18%)
  other arithmetic  57.4 us (15%)
  between operations  14 us (4%)
  local copies, waits for them, and re-layouts  4.73 us (1%)
    all_gather x2, waiting for transfers between devices, entering(): gathered = jax.tree.map(lambda a: lax.all_gather(a, axis), part)  211 us
    all_gather x2, blocking collectives, entering(): gathered = jax.tree.map(lambda a: lax.all_gather(a, axis), part)  62.3 us
    add x15, other arithmetic, compose_maps(): return (later[0] * earlier[0], later[0] * earlier[1] + later[1])  23.9 us
    all_gather x1, waiting for transfers between devices, body(): piece = lax.all_gather(table, 'doc', axis=0, tiled=True)  17.2 us
    add x16, other arithmetic, forward_step(): return (filt_var + drift_var, (gain_now, filt_var))  11.3 us
    all_gather x2, blocking collectives, joined(): everything = jax.tree.map(lambda part: lax.all_gather(part, axis), value)  9.41 us
    reduce_scatter x1, waiting for transfers between devices, body(): lax.psum_scatter(jnp.dot(marks, flat_weighted, preferred_element_type=jnp...  7.95 us
  transfers between devices with their start and end apart: 4, of which 4 were waited for; matrix products, arithmetic and copies ran while one was open for 5% of the time, Pallas kernels for 0%

commit v1 on v0

--- a/solution.py
+++ b/solution.py
@@ -7,6 +7,18 @@
 BLOCK = 128
 EITERS = 4
 init_variance = 4.0
+
+
+def gather_by_bits(shard, axis, dim):
+    ways, here = (lax.axis_size(axis), lax.axis_index(axis))
+    grown, reach = (shard, 1)
+    while reach < ways:
+        theirs = lax.ppermute(grown, axis, [(d, d ^ reach) for d in range(ways)])
+        mine_first = jnp.concatenate([grown, theirs], axis=dim)
+        theirs_first = jnp.concatenate([theirs, grown], axis=dim)
+        grown = jnp.where(here & reach == 0, mine_first, theirs_first)
+        reach = 2 * reach
+    return grown
 
 
 def joined(value, axis, combine):
@@ -105,7 +117,7 @@
     columns = jnp.sum(jnp.where(block_match, block_slot, 0), axis=-1) * BLOCK + slot_ids % BLOCK
     flat_columns = columns.reshape(-1)
     slot_total = flat_columns.shape[0]
-    piece = lax.all_gather(table, "doc", axis=0, tiled=True)
+    piece = gather_by_bits(table, "doc", 0)
     inside = (flat_columns >= 0) & (flat_columns < piece.shape[0])
     picked = jnp.take(piece, jnp.clip(flat_columns, 0, piece.shape[0] - 1), axis=0)
     looked = jnp.where(inside[:, None], picked, jnp.zeros_like(picked)).reshape(

time: 389 us -> 374 us (0.961)
  other arithmetic: 57.4 us -> 48.3 us
  waiting for transfers between devices: 236 us -> 230 us
    all_gather x1 -> x0, waiting for transfers between devices: 17.2 us -> none  [body(): piece = lax.all_gather(table, 'doc', axis=0, tiled=True)]
    ppermute x0 -> x1, waiting for transfers between devices: none -> 9.06 us  [gather_by_bits(): theirs = lax.ppermute(grown, axis, [(d, d ^ reach) for d in range(ways)])]
  transfers between devices with their start and end apart: 4 -> 4, of which waited for: 4 -> 4; matrix products, arithmetic and copies ran while one was open for 5% -> 4% of each run, Pallas kernels for 0% -> 0%
where the time goes in v1:
time: 374 us; the launch traced here: 373 us
  waiting for transfers between devices  230 us (61%)
  blocking collectives  71.7 us (19%)
  other arithmetic  48.3 us (13%)
  between operations  14.1 us (4%)
  local copies, waits for them, and re-layouts  3.75 us (1%)
    all_gather x2, waiting for transfers between devices, entering(): gathered = jax.tree.map(lambda a: lax.all_gather(a, axis), part)  211 us
    all_gather x2, blocking collectives, entering(): gathered = jax.tree.map(lambda a: lax.all_gather(a, axis), part)  62.3 us
    add x15, other arithmetic, compose_maps(): return (later[0] * earlier[0], later[0] * earlier[1] + later[1])  23.9 us
    add x16, other arithmetic, forward_step(): return (filt_var + drift_var, (gain_now, filt_var))  11.3 us
    reduce_scatter x1, waiting for transfers between devices, body(): lax.psum_scatter(jnp.dot(marks, flat_weighted, preferred_element_type=jnp...  9.44 us
    all_gather x2, blocking collectives, joined(): everything = jax.tree.map(lambda part: lax.all_gather(part, axis), value)  9.41 us
    ppermute x1, waiting for transfers between devices, gather_by_bits(): theirs = lax.ppermute(grown, axis, [(d, d ^ reach) for d in range(ways)])  9.06 us
  transfers between devices with their start and end apart: 4, of which 4 were waited for; matrix products, arithmetic and copies ran while one was open for 4% of the time, Pallas kernels for 0%

profile of v1, /device:TPU:0, one launch (start us, length us, event | category | flops | bytes accessed | tf_op | source)
XLA Modules:
  0.0 372.9 jit_solution(8513320098338110711)
XLA Ops:
  10.4 5.2 %all-gather.8 = f32[2,1,128]{2,1,0:T(1,128)S(1)} all-gather(f32[1,1,128]{2,1,0:T(1,128)S(1)} %bitcast.211), channel_id=4, replica_groups=mesh['tm'=16,'doc'=2] {'doc'}, dimensions={0}, use_global_device_ids=true | all-gather | bytes 1536 | tf_op jit(solution)/shard_map/all_gather | solution.py:25
  15.5 4.2 %all-gather.7 = f32[2,1,128]{2,1,0:T(1,128)S(1)} all-gather(f32[1,1,128]{2,1,0:T(1,128)S(1)} %bitcast.210), channel_id=3, replica_groups=mesh['tm'=16,'doc'=2] {'doc'}, dimensions={0}, use_global_device_ids=true | all-gather | bytes 1536 | tf_op jit(solution)/shard_map/all_gather | solution.py:25
  19.9 2.1 collective-permute-start
  22.5 9.1 %collective-permute-done = bf16[2048,128]{1,0:T(8,128)(2,1)S(1)} collective-permute-done((bf16[2048,128]{1,0:T(8,128)(2,1)S(1)}, bf16[2048,128]{1,0:T(8,128)(2,1)S(1)}, u32[]{:S(2)}, u32[]{:S(2)}) %collective-permute-start) | collective-permute-done | bytes 524320 | tf_op jit(solution)/shard_map/ppermute | solution.py:16
  36.8 2.4 fusion.2
  39.3 12.5 %while.49 = (s32[]{:T(128)}, f32[128]{0:T(128)S(1)}, f32[16,128]{1,0:T(8,128)S(1)}, f32[16,128]{1,0:T(8,128)S(1)}, f32[16,128]{1,0:T(8,128)}, /*index=5*/f32[128]{0:T(128)S(1)}, s32[]{:T(128)}, s32[]{:T(128)}) while((s32[]{:T(128)}, f32[128]{0:T(128)S(1)}, f32[16,128]{1,0:T(8,128)S(1)}, f32[16,128]{1,0:T(8,128)S(1)}, ...), condition=%wide.region_1.0_spmd.clone, body=%wide.region_0.0_spmd.clone.sunk | while | flops 771 | bytes 5235 | solution.py:59
  51.8 9.4 %reduce-scatter.2.cloned.1.call-done = bf16[2048,128]{1,0:T(8,128)(2,1)} async-done(((bf16[4096,128]{1,0:T(8,128)(2,1)}), bf16[2048,128]{1,0:T(8,128)(2,1)}) %reduce-scatter.2.cloned.1.call-update) | async-done | bytes 524304 | tf_op jit(solution)/shard_map/reduce_scatter | solution.py:130
  61.3 2.4 fusion.7
  63.8 21.7 %all-gather.6 = f32[16,1,128]{2,1,0:T(1,128)S(1)} all-gather(f32[1,1,128]{2,1,0:T(1,128)S(1)} %get-tuple-element.251), channel_id=1, replica_groups=mesh['tm'=16,'doc'=2] {'tm'}, dimensions={0}, use_global_device_ids=true | all-gather | bytes 8704 | tf_op jit(solution)/shard_map/all_gather | solution.py:38
  85.5 105.0 %all-gather.12.cloned.1.call-done = f32[32768,128]{1,0:T(8,128)} async-done(((f32[2048,128]{1,0:T(8,128)}), f32[32768,128]{1,0:T(8,128)}) %all-gather.12.cloned.1.call-update) | async-done | bytes 16777232 | tf_op jit(solution)/shard_map/all_gather | solution.py:38
  192.9 40.6 %all-gather.5 = f32[16,1,128]{2,1,0:T(1,128)S(1)} all-gather(f32[1,1,128]{2,1,0:T(1,128)S(1)} %bitcast.209), channel_id=2, replica_groups=mesh['tm'=16,'doc'=2] {'tm'}, dimensions={0}, use_global_device_ids=true | all-gather | bytes 8704 | tf_op jit(solution)/shard_map/all_gather | solution.py:38
  234.5 106.2 %all-gather.14.cloned.1.call-done = f32[32768,128]{1,0:T(8,128)} async-done(((f32[2048,128]{1,0:T(8,128)}), f32[32768,128]{1,0:T(8,128)}) %all-gather.14.cloned.1.call-update) | async-done | bytes 16777232 | tf_op jit(solution)/shard_map/all_gather | solution.py:38
  340.8 24.5 %while.48 = (s32[]{:T(128)}, f32[2048,128]{1,0:T(8,128)S(1)}, s32[]{:T(128)}, f32[16,128]{1,0:T(8,128)S(1)}, f32[16,2048,128]{2,1,0:T(8,128)}, /*index=5*/s32[]{:T(128)}, s32[]{:T(128)}, s32[]{:T(128)}, s32[]{:T(128)}) while((s32[]{:T(128)}, f32[2048,128]{1,0:T(8,128)S(1)}, s32[]{:T(128)}, f32[16,128]{1,0:T(8,128)S(1)}, ...), condition=%wide.region_21.22_spmd, body=%wide.region_20.21_spmd.sunk | while | flops 524294 | bytes 3147419 | solution.py:47
  340.8 1.7 bitcast_add_fusion.8
  342.6 1.6 bitcast_add_fusion.8
  344.2 1.6 bitcast_add_fusion.8
  345.8 1.6 bitcast_add_fusion.8
  350.7 1.6 bitcast_add_fusion.8
  352.3 1.6 bitcast_add_fusion.8
  353.9 1.6 bitcast_add_fusion.8
  355.5 1.6 bitcast_add_fusion.8
  357.2 1.6 bitcast_add_fusion.8
  360.4 1.6 bitcast_add_fusion.8
  362.0 1.6 bitcast_add_fusion.8
  (136 shorter events, 32.3 us)
Async XLA Ops:
  7.2 12.6 %copy-start = (f32[1,2048,128]{2,1,0:T(8,128)S(1)}, f32[1,2048,128]{2,1,0:T(8,128)}, u32[]{:S(2)}) copy-start(f32[1,2048,128]{2,1,0:T(8,128)} %param.13) | copy-start | bytes 3145732
  7.2 14.8 %copy-start.3 = (s32[1,4,128]{2,1,0:T(4,128)S(1)}, s32[1,4,128]{2,1,0:T(4,128)}, u32[]{:S(2)}) copy-start(s32[1,4,128]{2,1,0:T(4,128)} %param.14) | copy-start | bytes 6148
  7.2 14.8 %copy-start.7 = (s32[32]{0:T(128)S(1)}, s32[32]{0:T(128)}, u32[]{:S(2)}) copy-start(s32[32]{0:T(128)} %param.16) | copy-start | bytes 388
  7.2 15.0 %copy-start.6 = (s32[1,4,128]{2,1,0:T(4,128)S(1)}, s32[1,4,128]{2,1,0:T(4,128)}, u32[]{:S(2)}) copy-start(s32[1,4,128]{2,1,0:T(4,128)} %param.15) | copy-start | bytes 6148
  7.2 15.2 %copy-start.5 = (f32[128]{0:T(128)S(1)}, f32[128]{0:T(128)}, u32[]{:S(2)}) copy-start(f32[128]{0:T(128)} %param.17) | copy-start | bytes 1540
  7.2 54.1 %reduce-scatter.2.cloned.1.call-start = ((), (), s32[]{:S(2)}) async-start(), calls=%async_computation.1 | async-start | bytes 1572864 | tf_op jit(solution)/shard_map/reduce_scatter | solution.py:130
  19.9 11.7 %collective-permute-start = (bf16[2048,128]{1,0:T(8,128)(2,1)S(1)}, bf16[2048,128]{1,0:T(8,128)(2,1)S(1)}, u32[]{:S(2)}, u32[]{:S(2)}) collective-permute-start(bf16[2048,128]{1,0:T(8,128)(2,1)S(1)} %fusion.6), channel_id=1, source_target_pairs={{0,1},{1,0},{2,3},{3,2},{4,5},{5,4},{6,7},{7,6},{8,9},{9,8},{10,11... | collective-permute-start | bytes 1572872 | tf_op jit(solution)/shard_map/ppermute | solution.py:16
  36.8 2.5 copy-start.4
  39.3 151.2 %all-gather.12.cloned.1.call-start = ((), (), s32[]{:S(2)}) async-start(), calls=%async_computation.2 | async-start | bytes 17825792 | tf_op jit(solution)/shard_map/all_gather | solution.py:38
  63.7 277.0 %all-gather.14.cloned.1.call-start = ((), (), s32[]{:S(2)}) async-start(), calls=%async_computation.3 | async-start | bytes 17825792 | tf_op jit(solution)/shard_map/all_gather | solution.py:38
  190.6 1.2 copy-start.2
  340.8 24.5 %copy-start.1 = (f32[2048,128]{1,0:T(8,128)S(1)}, f32[2048,128]{1,0:T(8,128)}, u32[]{:S(2)}) copy-start(f32[2048,128]{1,0:T(8,128)} %add_multiply_fusion) | copy-start | bytes 3145732
Sparse Core Ops, SparseCore 0:
  39.4 21.8 reduce-scatter.1
  64.0 126.4 all-gather.11
  193.3 147.4 all-gather.13
